TPU v7x, 512 devices: a whole 4x4x16 slice. The times are simulated.
512 devices in a mesh: dir: 8 (over z_lo), row: 64 (over x, y, z_hi, core).
Axes of the slice: x: 4, y: 4, z: 16 (z_hi: 2, z_lo: 8; z = z_hi * 8 + z_lo), core: 2. Of those that a mesh axis runs over, the one named last changes fastest.
Arguments:
- white_noise: bfloat16 [2, 8192, 8192], P(None, ('dir', 'row')), may hold values from -6 to 6
- geometry: int32 [8, 2], P('dir'), may hold values from 0 to 3
- window: int32 [8], P('dir'), may hold values from 1 to 8, as said below
- tile_map: int32 [8, 8192], P('dir'), may hold values from 0 to 65535
- link_gain: float32 [8, 8192], P('dir'), may hold values from 0.1 to 1
- serving: int32 [8192], replicated, may hold values from 0 to 7
Outputs:
- fluctuation: float32 [8, 512, 128], P('dir', 'row')
- signal_ratio: float32 [8192], P(('dir', 'row'))
Inputs may be any that keep to these rules, and one draw needn't show every extreme that they name: geometry[d,0] is direction d's Fresnel-scale bin and geometry[d,1] its slant bin. `window`: some direction has the half-width 8. `tile_map`: tile (t,u) is numbered t * 128 + u.
All inputs are finite; a program needn't handle non-finite values.
Results may differ from a plain program's by a relative error of at most 0.034.
Values may be sent and summed in bfloat16 or wider, within the bound.
No kernel may reach another device: no remote copies, remote signals or barrier semaphores. Data moves between devices by JAX's collectives and lax.ppermute only.
A program may use at most 64 MiB of HBM per device.

v0:
```python
import math
import jax
import jax.numpy as jnp
from jax import lax
from jax.sharding import PartitionSpec as P

N = 8192
FIRST = 64
SECOND = 128
ROWS_DEV = 32
XTILES = 128
YTILES = 8
TILE_X = 64
full_turn = 2.0 * math.pi
noise_floor = 0.05
tiny_value = 1e-06
strength = 1.6
row_patterns = (
    "zrab,zwak->wrkb",
    "zrkb,zwbc->wrkc",
    "zrkc,wzbc->wrkb",
    "zrkb,wzak->wrab",
    "zrkb,zak->rab",
)
column_patterns = (
    "zaby,zwak->wkby",
    "zkby,zwbc->wkcy",
    "zkcy,wzbc->wkby",
    "zkby,wzak->waby",
    "zkby,zak->aby",
)


def complex_block(real_part, imag_part):
    return jnp.stack(
        [jnp.stack([real_part, imag_part]), jnp.stack([-imag_part, real_part])]
    ).astype(jnp.bfloat16)


def transform_tables(first, second):
    total = first * second
    outer_ids = jnp.arange(first, dtype=jnp.int32)
    inner_ids = jnp.arange(second, dtype=jnp.int32)
    outer_angle = (outer_ids[:, None] * outer_ids[None, :] % first).astype(jnp.float32) * (
        full_turn / first
    )
    inner_angle = (inner_ids[:, None] * inner_ids[None, :] % second).astype(jnp.float32) * (
        full_turn / second
    )
    twist_angle = (outer_ids[:, None] * inner_ids[None, :] % total).astype(jnp.float32) * (
        full_turn / total
    )
    return (
        complex_block(jnp.cos(outer_angle), -jnp.sin(outer_angle)),
        complex_block(jnp.cos(inner_angle), -jnp.sin(inner_angle)),
        jnp.cos(twist_angle),
        -jnp.sin(twist_angle),
    )


def signed_wave(positions, first, second):
    total = first * second
    wave_number = positions // second + first * (positions % second)
    return jnp.where(wave_number >= total // 2, wave_number - total, wave_number).astype(
        jnp.float32
    )


def spectral_filter(row_ids, column_ids):
    wave_rows = signed_wave(row_ids, FIRST, SECOND)
    wave_columns = signed_wave(column_ids, FIRST, SECOND)
    squared_radius = 16.0 + wave_rows[:, None] ** 2 + wave_columns[None, :] ** 2
    return strength * float(N) * float(N) * squared_radius ** (-0.75)


def fresnel_factor(geometry_row, first, second):
    total = first * second
    fresnel_area = 144.0 * jnp.exp2(geometry_row[0].astype(jnp.float32))
    positions = jnp.arange(total, dtype=jnp.int32).reshape(first, second)
    scaled = signed_wave(positions, first, second) * (full_turn / total)
    turning = 0.5 * scaled * scaled * fresnel_area
    return (jnp.cos(turning), -jnp.sin(turning))


def complex_times(values, real_part, imag_part):
    return jnp.stack(
        [
            values[0] * real_part - values[1] * imag_part,
            values[0] * imag_part + values[1] * real_part,
        ]
    )


def contract(pattern, operand, matrix):
    return jnp.einsum(pattern, operand, matrix, preferred_element_type=jnp.float32)


def table_length(tables):
    return tables[0].shape[2] * tables[1].shape[2]


def forward_axis(values, tables, factor, patterns, trailing):
    outer_table, inner_table, twist_real, twist_imag = tables
    factor_real, factor_imag = factor
    if trailing:
        twist_real, twist_imag = (twist_real[..., None], twist_imag[..., None])
        factor_real, factor_imag = (factor_real[..., None], factor_imag[..., None])
    section_one = complex_times(
        contract(patterns[0], values, outer_table), twist_real, twist_imag
    ).astype(jnp.bfloat16)
    section_two = contract(patterns[1], section_one, inner_table)
    return complex_times(section_two, factor_real, factor_imag).astype(jnp.bfloat16)


def inverse_first(values, tables, patterns, trailing):
    outer_table, inner_table, twist_real, twist_imag = tables
    if trailing:
        twist_real, twist_imag = (twist_real[..., None], twist_imag[..., None])
    return complex_times(
        contract(patterns[2], values, inner_table), twist_real, -twist_imag
    ).astype(jnp.bfloat16)


def inverse_axis(values, tables, patterns, trailing):
    section_one = inverse_first(values, tables, patterns, trailing)
    return contract(patterns[3], section_one, tables[0]) * (1.0 / table_length(tables))


def window_matrix(half_width):
    positions = jnp.arange(XTILES, dtype=jnp.int32)
    difference = (positions[:, None] - positions[None, :]) % XTILES
    distance = jnp.minimum(difference, XTILES - difference)
    return (distance <= half_width).astype(jnp.float32)


def tile_statistics(first_moment, second_moment, half_width, tile_rows):
    window_mask = window_matrix(half_width)
    cells = ((2 * half_width + 1) * (TILE_X * tile_rows)).astype(jnp.float32)
    mean_one = jnp.dot(first_moment, window_mask, precision=lax.Precision.HIGHEST) / cells
    mean_two = jnp.dot(second_moment, window_mask, precision=lax.Precision.HIGHEST) / cells
    fluctuation = mean_two / (mean_one * mean_one + tiny_value) - 1.0
    return (fluctuation, mean_one * jnp.exp(-fluctuation))


def turn_pair(angle):
    quarter = jnp.round(angle * (2.0 / 3.141592653589793))
    rest = angle - quarter * 1.5703125
    rest = rest - quarter * 0.0004837512969970703
    rest = rest - quarter * 7.549789954891882e-08
    square = rest * rest
    sine = rest + rest * square * (
        -0.16666654611 + square * (0.0083321608736 + square * -0.00019515295891)
    )
    cosine = (
        1.0
        - 0.5 * square
        + square
        * square
        * (0.04166664568298827 + square * (-0.001388731625493765 + square * 2.443315711809948e-05))
    )
    turn = quarter.astype(jnp.int32) & 3
    swap = turn & 1 == 1
    sin_value = jnp.where(swap, cosine, sine)
    cos_value = jnp.where(swap, sine, cosine)
    sin_value = jnp.where(turn >= 2, -sin_value, sin_value)
    cos_value = jnp.where((turn == 1) | (turn == 2), -cos_value, cos_value)
    return (cos_value, sin_value)


def propagate_columns(phase_patch, tables_y, slant_factor, fresnel_y):
    patch_rows = phase_patch.shape[0]
    width_here = phase_patch.shape[1]
    outer_len = tables_y[0].shape[2]
    inner_len = tables_y[1].shape[2]
    turned_phase = slant_factor * phase_patch
    screen_field = jnp.stack(turn_pair(turned_phase)).astype(jnp.bfloat16)
    stacked = screen_field.reshape(2, outer_len, inner_len, width_here)
    spectral = forward_axis(stacked, tables_y, fresnel_y, column_patterns, True)
    result = inverse_axis(spectral, tables_y, column_patterns, True)
    return result.astype(jnp.bfloat16).reshape(2, patch_rows, width_here)


def body(white_noise, geometry, window, tile_map, link_gain, serving):
    row_count = lax.axis_size("row")
    tables = transform_tables(FIRST, SECOND)
    tables_y = transform_tables(row_count, ROWS_DEV)
    patch_len = row_count * ROWS_DEV
    rows_here = white_noise.shape[1]
    row_start = lax.axis_index(("dir", "row")) * rows_here
    row_ids = row_start + jnp.arange(rows_here, dtype=jnp.int32)
    column_ids = jnp.arange(N, dtype=jnp.int32)
    spectral_gain = spectral_filter(row_ids, column_ids)
    spectrum = (white_noise.astype(jnp.float32) * spectral_gain).astype(jnp.bfloat16)
    section_first = inverse_first(
        spectrum.reshape(2, rows_here, FIRST, SECOND), tables, row_patterns, False
    )
    half_screen = contract("zrkb,wzak->awrb", section_first, tables[0]) * (1.0 / N)
    half_screen = half_screen.astype(jnp.bfloat16)
    turned = lax.all_to_all(half_screen, "row", split_axis=0, concat_axis=0, tiled=True)
    slant_factor = 1.0 + 0.25 * geometry[0, 1].astype(jnp.float32)
    fresnel_x = fresnel_factor(geometry[0], FIRST, SECOND)
    fresnel_y = fresnel_factor(geometry[0], row_count, ROWS_DEV)
    offset_rows = N // 4 * geometry[0, 1]
    columns = SECOND
    blocks = row_count * rows_here // SECOND
    split = SECOND // rows_here
    block_start = lax.axis_index("dir") * blocks
    stacked = turned.reshape(blocks, split, 2, rows_here, columns)
    inner_split = tables[1].reshape(2, 2, SECOND, split, rows_here)
    twist_real = lax.dynamic_slice_in_dim(tables[2], block_start, blocks, 0)[..., None]
    twist_imag = lax.dynamic_slice_in_dim(tables[3], block_start, blocks, 0)[..., None]
    section_one = complex_times(
        contract("khzrx,wzbhr->wkbx", stacked, inner_split), twist_real, -twist_imag
    )
    section_one = section_one.astype(jnp.bfloat16)
    outer_count = patch_len // SECOND
    outer_ids = (offset_rows // SECOND + jnp.arange(outer_count, dtype=jnp.int32)) % FIRST
    patch_outer = jnp.take(tables[0][0], outer_ids, axis=1)
    gathered = lax.all_gather(section_one, "dir", axis=1, tiled=True)
    depth = gathered.shape[0] * gathered.shape[1]
    patch_matrix = jnp.transpose(patch_outer, (1, 0, 2)).reshape(outer_count, depth)
    phase_patch = jnp.dot(
        patch_matrix, gathered.reshape(depth, -1), preferred_element_type=jnp.float32
    )
    phase_patch = phase_patch.reshape(patch_len, columns) * (1.0 / N)
    screen_field = propagate_columns(phase_patch, tables_y, slant_factor, fresnel_y)
    stacked_field = screen_field.reshape(2, row_count, ROWS_DEV, columns)
    portion = lax.all_to_all(stacked_field, "row", split_axis=1, concat_axis=3, tiled=True)
    item_count = portion.shape[2]
    stacked = portion.reshape(2, item_count, FIRST, SECOND)
    spectral = forward_axis(stacked, tables, fresnel_x, row_patterns, False)
    wave_field = inverse_axis(spectral, tables, row_patterns, False)
    intensity = wave_field[0] * wave_field[0] + wave_field[1] * wave_field[1]
    intensity = intensity.reshape(item_count, XTILES, TILE_X)
    tile_one = jnp.sum(intensity, axis=2)
    tile_two = jnp.sum(intensity * intensity, axis=2)
    tile_rows = ROWS_DEV // YTILES
    first_moment = jnp.sum(tile_one.reshape(YTILES, tile_rows, XTILES), axis=1)
    second_moment = jnp.sum(tile_two.reshape(YTILES, tile_rows, XTILES), axis=1)
    fluctuation, faded_power = tile_statistics(first_moment, second_moment, window[0], tile_rows)
    tile_total = faded_power.shape[0] * faded_power.shape[1]
    local_tile = tile_map[0] - lax.axis_index("row") * tile_total
    inside = (local_tile >= 0) & (local_tile < tile_total)
    tile_row = local_tile // XTILES
    tile_column = local_tile % XTILES
    pick_row = (tile_row[:, None] == jnp.arange(YTILES, dtype=jnp.int32)[None, :]).astype(
        jnp.float32
    )
    row_values = jnp.dot(pick_row, faded_power, precision=lax.Precision.HIGHEST)
    pick_column = tile_column[:, None] == jnp.arange(XTILES, dtype=jnp.int32)[None, :]
    looked = jnp.sum(jnp.where(pick_column, row_values, 0.0), axis=1)
    looked = jnp.where(inside, looked, 0.0)
    received = link_gain[0] * looked
    direction = lax.axis_index("dir")
    serves_here = serving == direction
    signal_part = jnp.where(serves_here, received, 0.0)
    interference_part = jnp.where(serves_here, 0.0, received)
    dir_count = lax.axis_size("dir")
    share_size = serving.shape[0] // (dir_count * row_count)
    parts = jnp.stack([signal_part, interference_part]).reshape(2, dir_count, row_count, share_size)
    parts = lax.all_to_all(parts, "row", split_axis=2, concat_axis=2, tiled=True)
    parts = jnp.sum(parts, axis=2, keepdims=True)
    parts = lax.all_to_all(parts, "dir", split_axis=1, concat_axis=1, tiled=True)
    parts = jnp.sum(parts, axis=(1, 2))
    signal, interference = (parts[0], parts[1])
    signal_ratio = jnp.log10(signal / (interference + noise_floor))
    return (fluctuation[None], signal_ratio)


def solution(mesh):
    return jax.shard_map(
        body,
        mesh=mesh,
        in_specs=(
            P(None, ("dir", "row"), None),
            P("dir", None),
            P("dir"),
            P("dir", None),
            P("dir", None),
            P(),
        ),
        out_specs=(P("dir", "row", None), P(("dir", "row"))),
        check_vma=False,
    )
```

profile of v0, /device:TPU:1, one launch (start us, length us, event | category | flops | bytes accessed | tf_op | source)
XLA Modules:
  0.0 306.3 jit_solution(62604927626251971)
XLA Ops:
  7.2 0.2 negate_convert_fusion.2
  7.3 0.1 fusion.136
  7.5 0.3 negate_convert_fusion.1
  7.8 0.3 fusion.106
  8.0 0.1 fusion.130
  8.2 0.3 power_multiply_fusion
  8.5 1.1 multiply_convert_fusion
  9.7 0.1 copy.179
  9.8 0.3 convolution_bitcast_fusion.8
  10.2 0.2 subtract_convert_fusion.7
  10.3 0.3 fusion.7
  10.7 1.1 copy.128
  11.8 22.2 %all-to-all-start = ((bf16[64,2,16,128]{3,2,1,0:T(8,128)(2,1)}), bf16[64,2,16,128]{3,2,1,0:T(8,128)(2,1)S(1)}, u32[]{:S(2)}, u32[]{:S(2)}) async-start(bf16[64,2,16,128]{3,2,1,0:T(8,128)(2,1)} %copy.128), calls=%async_computation | async-start | bytes 1048576 | tf_op jit(solution)/shard_map/all_to_all | solution.py:199
  34.1 0.2 all-gather.2.cloned.1.call-start
  34.3 0.1 fusion.141
  34.5 0.3 negate_convert_fusion
  34.8 21.1 %all-to-all-done = bf16[64,2,16,128]{3,2,1,0:T(8,128)(2,1)S(1)} async-done(((bf16[64,2,16,128]{3,2,1,0:T(8,128)(2,1)}), bf16[64,2,16,128]{3,2,1,0:T(8,128)(2,1)S(1)}, u32[]{:S(2)}, u32[]{:S(2)}) %all-to-all-start) | async-done | bytes 524320 | tf_op jit(solution)/shard_map/all_to_all | solution.py:199
  55.9 0.3 convolution_bitcast_fusion.7
  56.2 0.3 subtract_convert_fusion.6
  56.6 0.8 pad_maximum_fusion.7
  57.5 0.6 fusion.173
  59.4 0.6 gather_fusion
  60.9 0.1 sine_negate_fusion.1
  61.2 0.1 fusion.146
  61.6 105.1 %all-gather.2.cloned.1.call-done = bf16[2,64,128,128]{3,2,1,0:T(8,128)(2,1)} async-done(((bf16[2,8,128,128]{3,2,1,0:T(8,128)(2,1)}), bf16[2,64,128,128]{3,2,1,0:T(8,128)(2,1)}) %all-gather.2.cloned.1.call-update) | async-done | bytes 4194320 | tf_op jit(solution)/shard_map/all_gather | solution.py:219
  166.7 4.5 %convolution_multiply_fusion = f32[16,16384]{1,0:T(8,128)S(1)} fusion(bf16[16,128]{1,0:T(8,128)(2,1)S(1)} %reshape.886, bf16[16,8,128,128]{3,2,1,0:T(8,128)(2,1)} %bitcast.201, f32[]{:T(128)} %bitcast.39), kind=kOutput, calls=%fused_computation.1 | convolution fusion | flops 67371008 | bytes 5246980 | tf_op jit(solution)/shard_map/dot_general | solution.py:222
  171.2 0.2 mul.1413
  171.4 1.6 fusion.18
  173.0 0.5 convolution_bitcast_fusion.5
  173.4 0.7 subtract_convert_fusion.5
  174.2 0.1 pad_maximum_fusion
  174.3 0.9 convolution_bitcast_fusion.4
  175.2 0.7 subtract_convert_fusion.4
  175.9 0.5 convolution_bitcast_fusion.3
  176.3 1.2 copy.255
  177.5 0.7 subtract_convert_fusion.3
  178.3 0.5 fusion.3
  178.8 1.7 copy.139
  180.4 11.7 %all-to-all-start.1 = ((bf16[2,64,32,128]{3,2,0,1:T(8,128)(2,1)}), bf16[2,64,32,128]{3,2,0,1:T(8,128)(2,1)S(1)}, u32[]{:S(2)}, u32[]{:S(2)}) async-start(bf16[2,64,32,128]{3,2,0,1:T(8,128)(2,1)} %copy.139), calls=%async_computation.1 | async-start | bytes 2097152 | tf_op jit(solution)/shard_map/all_to_all | solution.py:228
  192.8 0.2 sine_negate_fusion
  193.1 53.6 %all-to-all-done.1 = bf16[2,64,32,128]{3,2,0,1:T(8,128)(2,1)S(1)} async-done(((bf16[2,64,32,128]{3,2,0,1:T(8,128)(2,1)}), bf16[2,64,32,128]{3,2,0,1:T(8,128)(2,1)S(1)}, u32[]{:S(2)}, u32[]{:S(2)}) %all-to-all-start.1) | async-done | bytes 1048608 | tf_op jit(solution)/shard_map/all_to_all | solution.py:228
  246.6 0.9 convolution_bitcast_fusion.2
  247.5 0.3 subtract_convert_fusion.2
  247.8 0.4 convolution_bitcast_fusion.1
  248.3 0.3 subtract_convert_fusion.1
  248.6 0.5 convolution_bitcast_fusion
  249.1 0.3 subtract_convert_fusion
  249.4 0.5 fusion.2
  249.9 0.2 fusion.20
  250.1 0.3 add.655
  250.4 1.1 fusion.172
  251.6 0.2 convolution_divide_fusion
  251.8 0.2 fusion.8
  252.0 2.3 fusion.4
  254.3 0.1 stack.177
  254.5 0.1 stack.176
  254.6 0.3 copy.256
  255.0 0.2 reshape.1063
  255.2 19.7 %all_to_all.30 = f32[64,1,256]{2,1,0:T(1,128)S(1)} all-to-all(f32[64,1,256]{2,1,0:T(1,128)S(1)} %reshape.1063), channel_id=1, replica_groups=mesh['dir'=8,'row'=64] {'row'}, dimensions={0} | all-to-all | bytes 131072 | tf_op jit(solution)/shard_map/all_to_all | solution.py:261
  274.9 0.5 broadcast.1677
  275.4 0.8 reduce
  276.2 0.2 reshape.1064
  276.5 22.5 %all_to_all.31 = f32[2,8,1,16]{3,0,2,1:T(2,128)S(1)} all-to-all(f32[2,8,1,16]{3,0,2,1:T(2,128)S(1)} %copy.149), channel_id=1, replica_groups=mesh['dir'=8,'row'=64] {'dir'}, dimensions={1} | all-to-all | bytes 2048 | tf_op jit(solution)/shard_map/all_to_all | solution.py:263
  299.0 0.5 multiply_bitcast_fusion
  (40 shorter events, 1.1 us)
Async XLA Ops:
  11.8 44.1 %all-to-all-start = ((bf16[64,2,16,128]{3,2,1,0:T(8,128)(2,1)}), bf16[64,2,16,128]{3,2,1,0:T(8,128)(2,1)S(1)}, u32[]{:S(2)}, u32[]{:S(2)}) async-start(bf16[64,2,16,128]{3,2,1,0:T(8,128)(2,1)} %copy.128), calls=%async_computation | async-start | bytes 1048576 | tf_op jit(solution)/shard_map/all_to_all | solution.py:199
  34.1 132.6 %all-gather.2.cloned.1.call-start = ((), (), s32[]{:S(2)}) async-start(), calls=%async_computation.4 | async-start | bytes 4718592 | tf_op jit(solution)/shard_map/all_gather | solution.py:219
  55.9 1.5 copy-start.3
  178.7 14.2 %copy-start.1 = (s32[1,8192]{1,0:T(1,128)S(1)}, s32[1,8192]{1,0:T(1,128)}, u32[]{:S(2)}) copy-start(s32[1,8192]{1,0:T(1,128)} %param.9) | copy-start | bytes 98308
  180.4 66.2 %all-to-all-start.1 = ((bf16[2,64,32,128]{3,2,0,1:T(8,128)(2,1)}), bf16[2,64,32,128]{3,2,0,1:T(8,128)(2,1)S(1)}, u32[]{:S(2)}, u32[]{:S(2)}) async-start(bf16[2,64,32,128]{3,2,0,1:T(8,128)(2,1)} %copy.139), calls=%async_computation.1 | async-start | bytes 2097152 | tf_op jit(solution)/shard_map/all_to_all | solution.py:228
  251.8 2.5 copy-start
  251.8 2.5 copy-start.2
  252.0 2.3 copy-start.4
Sparse Core Ops, SparseCore 0:
  57.6 109.0 all-gather.1
where the time goes:
time: 307 us; the launch traced here: 306 us
  waiting for transfers between devices  180 us (59%)
  blocking collectives  42.1 us (14%)
  starting transfers between devices  34.2 us (11%)
  between operations  17.2 us (6%)
  other arithmetic  12.8 us (4%)
  matrix products  12.6 us (4%)
  local copies, waits for them, and re-layouts  7.6 us (2%)
    all_gather x1, waiting for transfers between devices, body(): gathered = lax.all_gather(section_one, 'dir', axis=1, tiled=True)  105 us
    all_to_all x1, waiting for transfers between devices, body(): lax.all_to_all(stacked_field, 'row', split_axis=1, concat_axis=3, tiled=T...  53.6 us
    all_to_all x1, blocking collectives, body(): lax.all_to_all(parts, 'dir', split_axis=1, concat_axis=1, tiled=True)  22.5 us
    all_to_all x1, starting transfers between devices, body(): lax.all_to_all(half_screen, 'row', split_axis=0, concat_axis=0, tiled=True)  22.2 us
    all_to_all x1, waiting for transfers between devices, body(): lax.all_to_all(half_screen, 'row', split_axis=0, concat_axis=0, tiled=True)  21.1 us
    all_to_all x1, blocking collectives, body(): lax.all_to_all(parts, 'row', split_axis=2, concat_axis=2, tiled=True)  19.7 us
    all_to_all x1, starting transfers between devices, body(): lax.all_to_all(stacked_field, 'row', split_axis=1, concat_axis=3, tiled=T...  11.7 us
    another operation x16, other arithmetic  6.5 us
  transfers between devices with their start and end apart: 3, of which 3 were waited for; matrix products, arithmetic and copies ran while one was open for 1% of the time, Pallas kernels for 0%

commit v1 on v0

--- a/solution.py
+++ b/solution.py
@@ -1,8 +1,10 @@
+import functools
 import math
 import jax
 import jax.numpy as jnp
 from jax import lax
 from jax.sharding import PartitionSpec as P
+from jax.lax import all_to_all, axis_size
 
 N = 8192
 FIRST = 64
@@ -31,6 +33,17 @@
 )
 
 
+def wait_the_sums_all(block_in, dev_axis, ndim_at):
+    wide_out = jnp.concatenate(
+        all_to_all(jnp.stack(axis_size(dev_axis) * [block_in], axis=0), dev_axis, 0, 0),
+        axis=ndim_at,
+    )
+    return wide_out
+
+
+replace_the_column = functools.partial(wait_the_sums_all, dev_axis="dir", ndim_at=1)
+
+
 def complex_block(real_part, imag_part):
     return jnp.stack(
         [jnp.stack([real_part, imag_part]), jnp.stack([-imag_part, real_part])]
@@ -216,7 +229,7 @@
     outer_count = patch_len // SECOND
     outer_ids = (offset_rows // SECOND + jnp.arange(outer_count, dtype=jnp.int32)) % FIRST
     patch_outer = jnp.take(tables[0][0], outer_ids, axis=1)
-    gathered = lax.all_gather(section_one, "dir", axis=1, tiled=True)
+    gathered = replace_the_column(section_one)
     depth = gathered.shape[0] * gathered.shape[1]
     patch_matrix = jnp.transpose(patch_outer, (1, 0, 2)).reshape(outer_count, depth)
     phase_patch = jnp.dot(

time: 307 us -> 381 us (1.24)
  waiting for transfers between devices: 180 us -> 245 us
  starting transfers between devices: 34.2 us -> 48.8 us
  between operations: 17.2 us -> 3.8 us
  local copies, waits for them, and re-layouts: 7.6 us -> 13.1 us
  blocking collectives: 42.1 us -> 47.4 us
    all_to_all x0 -> x1, waiting for transfers between devices: none -> 181 us  [wait_the_sums_all(): all_to_all(jnp.stack(axis_size(dev_axis) * [block_in], axis=0), dev_axis,...]
    all_gather x1 -> x0, waiting for transfers between devices: 105 us -> none  [body(): gathered = lax.all_gather(section_one, 'dir', axis=1, tiled=True)]
    all_to_all x0 -> x1, starting transfers between devices: none -> 20.9 us  [wait_the_sums_all(): all_to_all(jnp.stack(axis_size(dev_axis) * [block_in], axis=0), dev_axis,...]
    all_to_all x1, blocking collectives: 19.7 us -> 30.9 us  [body(): lax.all_to_all(parts, 'row', split_axis=2, concat_axis=2, tiled=True)]
    all_to_all x1, waiting for transfers between devices: 53.6 us -> 42.6 us  [body(): lax.all_to_all(stacked_field, 'row', split_axis=1, concat_axis=3, tiled=T...]
    all_to_all x1, starting transfers between devices: 11.7 us -> 5.7 us  [body(): lax.all_to_all(stacked_field, 'row', split_axis=1, concat_axis=3, tiled=T...]
    all_to_all x1, blocking collectives: 22.5 us -> 16.5 us  [body(): lax.all_to_all(parts, 'dir', split_axis=1, concat_axis=1, tiled=True)]
where the time goes in v1:
time: 381 us
  waiting for transfers between devices  245 us (64%)
  starting transfers between devices  48.8 us (13%)
  blocking collectives  47.4 us (12%)
  local copies, waits for them, and re-layouts  13.1 us (3%)
  other arithmetic  12 us (3%)
  matrix products  10.5 us (3%)
    all_to_all x1, waiting for transfers between devices, wait_the_sums_all(): all_to_all(jnp.stack(axis_size(dev_axis) * [block_in], axis=0), dev_axis,...  181 us
    all_to_all x1, waiting for transfers between devices, body(): lax.all_to_all(stacked_field, 'row', split_axis=1, concat_axis=3, tiled=T...  42.6 us
    all_to_all x1, blocking collectives, body(): lax.all_to_all(parts, 'row', split_axis=2, concat_axis=2, tiled=True)  30.9 us
    all_to_all x1, starting transfers between devices, body(): lax.all_to_all(half_screen, 'row', split_axis=0, concat_axis=0, tiled=True)  22.2 us
    all_to_all x1, waiting for transfers between devices, body(): lax.all_to_all(half_screen, 'row', split_axis=0, concat_axis=0, tiled=True)  21.3 us
    all_to_all x1, starting transfers between devices, wait_the_sums_all(): all_to_all(jnp.stack(axis_size(dev_axis) * [block_in], axis=0), dev_axis,...  20.9 us
    all_to_all x1, blocking collectives, body(): lax.all_to_all(parts, 'dir', split_axis=1, concat_axis=1, tiled=True)  16.5 us
  transfers between devices with their start and end apart: 3, of which 3 were waited for; matrix products, arithmetic and copies ran while one was open for 1% of the time, Pallas kernels for 0%

profile of v1, /device:TPU:1, one launch (start us, length us, event | category | flops | bytes accessed | tf_op | source)
XLA Modules:
  0.0 380.9 jit_solution(10352149233500588817)
XLA Ops:
  0.6 0.2 negate_convert_fusion.2
  0.8 0.1 fusion.136
  1.0 0.3 negate_convert_fusion.1
  1.2 0.3 fusion.106
  1.5 0.1 fusion.130
  1.7 0.3 power_multiply_fusion
  2.0 1.1 multiply_convert_fusion
  3.1 0.1 copy.183
  3.3 0.3 convolution_bitcast_fusion.8
  3.6 0.2 subtract_convert_fusion.7
  3.8 0.3 fusion.7
  4.1 1.1 copy.131
  5.3 22.2 %all-to-all-start = ((bf16[64,2,16,128]{3,2,1,0:T(8,128)(2,1)}), bf16[64,2,16,128]{3,2,1,0:T(8,128)(2,1)S(1)}, u32[]{:S(2)}, u32[]{:S(2)}) async-start(bf16[64,2,16,128]{3,2,1,0:T(8,128)(2,1)} %copy.131), calls=%async_computation | async-start | bytes 1048576 | tf_op jit(solution)/shard_map/all_to_all | solution.py:212
  27.5 0.1 fusion.141
  27.7 0.3 negate_convert_fusion
  28.0 21.3 %all-to-all-done = bf16[64,2,16,128]{3,2,1,0:T(8,128)(2,1)S(1)} async-done(((bf16[64,2,16,128]{3,2,1,0:T(8,128)(2,1)}), bf16[64,2,16,128]{3,2,1,0:T(8,128)(2,1)S(1)}, u32[]{:S(2)}, u32[]{:S(2)}) %all-to-all-start) | async-done | bytes 524320 | tf_op jit(solution)/shard_map/all_to_all | solution.py:212
  49.4 0.3 convolution_bitcast_fusion.7
  49.7 0.3 subtract_convert_fusion.6
  50.1 3.0 stack.179
  53.1 20.9 %all-to-all-start.1 = ((bf16[8,2,8,128,128]{4,3,2,1,0:T(8,128)(2,1)}), bf16[8,2,8,128,128]{4,3,2,1,0:T(8,128)(2,1)}, u32[]{:S(2)}, u32[]{:S(2)}) async-start(bf16[8,2,8,128,128]{4,3,2,1,0:T(8,128)(2,1)} %stack.179), calls=%async_computation.1 | async-start | bytes 8388608 | tf_op jit(solution)/shard_map/all_to_all | solution.py:38
  74.0 0.6 fusion.173
  76.0 0.6 gather_fusion
  77.5 0.1 sine_negate_fusion.1
  78.1 181.4 %all-to-all-done.1 = bf16[8,2,8,128,128]{4,3,2,1,0:T(8,128)(2,1)} async-done(((bf16[8,2,8,128,128]{4,3,2,1,0:T(8,128)(2,1)}), bf16[8,2,8,128,128]{4,3,2,1,0:T(8,128)(2,1)}, u32[]{:S(2)}, u32[]{:S(2)}) %all-to-all-start.1) | async-done | bytes 4194336 | tf_op jit(solution)/shard_map/all_to_all | solution.py:38
  259.5 2.5 copy.132
  262.0 2.3 convolution_multiply_fusion
  264.3 0.2 mul.1413
  264.5 1.6 fusion.18
  266.1 0.5 convolution_bitcast_fusion.5
  266.6 0.7 subtract_convert_fusion.5
  267.3 0.1 pad_maximum_fusion
  267.4 0.9 convolution_bitcast_fusion.4
  268.3 0.7 subtract_convert_fusion.4
  269.0 0.5 convolution_bitcast_fusion.3
  269.5 1.2 copy.259
  270.7 0.7 subtract_convert_fusion.3
  271.4 0.5 fusion.3
  271.9 1.6 copy.143
  273.5 5.7 %all-to-all-start.2 = ((bf16[2,64,32,128]{3,2,0,1:T(8,128)(2,1)}), bf16[2,64,32,128]{3,2,0,1:T(8,128)(2,1)S(1)}, u32[]{:S(2)}, u32[]{:S(2)}) async-start(bf16[2,64,32,128]{3,2,0,1:T(8,128)(2,1)} %copy.143), calls=%async_computation.2 | async-start | bytes 2097152 | tf_op jit(solution)/shard_map/all_to_all | solution.py:241
  279.9 0.2 sine_negate_fusion
  280.2 42.6 %all-to-all-done.2 = bf16[2,64,32,128]{3,2,0,1:T(8,128)(2,1)S(1)} async-done(((bf16[2,64,32,128]{3,2,0,1:T(8,128)(2,1)}), bf16[2,64,32,128]{3,2,0,1:T(8,128)(2,1)S(1)}, u32[]{:S(2)}, u32[]{:S(2)}) %all-to-all-start.2) | async-done | bytes 1048608 | tf_op jit(solution)/shard_map/all_to_all | solution.py:241
  322.8 0.9 convolution_bitcast_fusion.2
  323.7 0.3 subtract_convert_fusion.2
  324.0 0.4 convolution_bitcast_fusion.1
  324.4 0.3 subtract_convert_fusion.1
  324.7 0.5 convolution_bitcast_fusion
  325.2 0.3 subtract_convert_fusion
  325.5 0.5 fusion.2
  326.0 0.2 fusion.20
  326.2 0.3 add.655
  326.6 1.1 fusion.172
  327.8 0.2 convolution_divide_fusion
  328.0 0.2 fusion.8
  328.1 2.3 fusion.4
  330.5 0.1 stack.188
  330.6 0.1 stack.187
  330.8 0.3 copy.260
  331.1 0.2 reshape.1070
  331.3 30.9 %all_to_all.35 = f32[64,1,256]{2,1,0:T(1,128)S(1)} all-to-all(f32[64,1,256]{2,1,0:T(1,128)S(1)} %reshape.1070), channel_id=1, replica_groups=mesh['dir'=8,'row'=64] {'row'}, dimensions={0} | all-to-all | bytes 131072 | tf_op jit(solution)/shard_map/all_to_all | solution.py:274
  362.3 0.5 broadcast.1678
  362.8 0.8 reduce
  363.6 0.2 reshape.1071
  363.9 16.5 %all_to_all.36 = f32[2,8,1,16]{3,0,2,1:T(2,128)S(1)} all-to-all(f32[2,8,1,16]{3,0,2,1:T(2,128)S(1)} %copy.153), channel_id=1, replica_groups=mesh['dir'=8,'row'=64] {'dir'}, dimensions={1} | all-to-all | bytes 2048 | tf_op jit(solution)/shard_map/all_to_all | solution.py:276
  380.4 0.5 multiply_bitcast_fusion
  (41 shorter events, 1.2 us)
Async XLA Ops:
  5.3 44.1 %all-to-all-start = ((bf16[64,2,16,128]{3,2,1,0:T(8,128)(2,1)}), bf16[64,2,16,128]{3,2,1,0:T(8,128)(2,1)S(1)}, u32[]{:S(2)}, u32[]{:S(2)}) async-start(bf16[64,2,16,128]{3,2,1,0:T(8,128)(2,1)} %copy.131), calls=%async_computation | async-start | bytes 1048576 | tf_op jit(solution)/shard_map/all_to_all | solution.py:212
  53.1 20.9 %copy-start.3 = (s32[1,2]{1,0:T(1,128)S(1)}, s32[1,2]{1,0:T(1,128)}, u32[]{:S(2)}) copy-start(s32[1,2]{1,0:T(1,128)} %param.7) | copy-start | bytes 28
  53.1 206.4 %all-to-all-start.1 = ((bf16[8,2,8,128,128]{4,3,2,1,0:T(8,128)(2,1)}), bf16[8,2,8,128,128]{4,3,2,1,0:T(8,128)(2,1)}, u32[]{:S(2)}, u32[]{:S(2)}) async-start(bf16[8,2,8,128,128]{4,3,2,1,0:T(8,128)(2,1)} %stack.179), calls=%async_computation.1 | async-start | bytes 8388608 | tf_op jit(solution)/shard_map/all_to_all | solution.py:38
  271.9 8.2 %copy-start.1 = (s32[1,8192]{1,0:T(1,128)S(1)}, s32[1,8192]{1,0:T(1,128)}, u32[]{:S(2)}) copy-start(s32[1,8192]{1,0:T(1,128)} %param.9) | copy-start | bytes 98308
  273.5 49.3 %all-to-all-start.2 = ((bf16[2,64,32,128]{3,2,0,1:T(8,128)(2,1)}), bf16[2,64,32,128]{3,2,0,1:T(8,128)(2,1)S(1)}, u32[]{:S(2)}, u32[]{:S(2)}) async-start(bf16[2,64,32,128]{3,2,0,1:T(8,128)(2,1)} %copy.143), calls=%async_computation.2 | async-start | bytes 2097152 | tf_op jit(solution)/shard_map/all_to_all | solution.py:241
  327.9 2.5 copy-start
  328.0 2.5 copy-start.2
  328.1 2.3 copy-start.4
